TPU v7x, 256 devices: a whole 4x4x8 slice. The times are simulated.
256 devices in a mesh: own: 32 (over x, z), row: 8 (over y, core).
Axes of the slice: x: 4, y: 4, z: 8, core: 2. Of those that a mesh axis runs over, the one named last changes fastest.
Arguments:
- sigma_anc: float32 [16384, 16384], P('row', 'own'), may hold values from -1.5 to 1.5
- row_blocks: int32 [64, 8], replicated, may hold values from 0 to 63, as said below
- panel1: float32 [64, 2048, 256], P('own', 'row'), may hold values from -0.375 to 0.375
- diag_inv1: float32 [64, 256, 256], P('own'), as said below
- mask1: int32 [64, 8], P('own', 'row'), may hold values 0 or 1
- parent_block2: float32 [64, 256, 256], P('own'), may hold values from -0.375 to 0.375
- panel2: float32 [64, 2048, 256], P('own', 'row'), may hold values from -0.375 to 0.375
- diag_inv2: float32 [64, 256, 256], P('own'), as said below
- mask2: int32 [64, 8], P('own', 'row'), may hold values 0 or 1
Outputs:
- sel1_panel: float32 [64, 2048, 256], P('own', 'row')
- sel1_diag: float32 [64, 256, 256], P('own')
- sel2_parent: float32 [64, 256, 256], P('own')
- sel2_panel: float32 [64, 2048, 256], P('own', 'row')
- sel2_diag: float32 [64, 256, 256], P('own')
Inputs may be any that keep to these rules, and one draw needn't show every extreme that they name: `row_blocks`: entry l of each row lies in block rows 8 * l to 8 * (l + 1) - 1; for supernodes s with the same s // 2, the entries of one column l lie in different aligned runs of 2 block rows. `diag_inv1`: lower triangular, with diagonal entries from 1 to 2. `diag_inv2`: lower triangular, with diagonal entries from 1 to 2.
All inputs are finite; a program needn't handle non-finite values. No bound on the sum of `mask1` or of `mask2` on one device may be relied on, other than what follows from the above.
Results may differ from a plain program's by a relative error of at most 0.000071.
Values sent between devices are 32-bit elements; how exact they have to be, the bound alone decides.
No kernel may reach another device: no remote copies, remote signals or barrier semaphores. Data moves between devices by JAX's collectives and lax.ppermute only.
A program may use at most 128 MiB of HBM per device.

v0:
```python
import jax
import jax.numpy as jnp
from jax import lax
from jax.sharding import PartitionSpec as P

B = 256
HIGH = lax.Precision.HIGHEST


def shifted(shard, axis, by):
    length = lax.axis_size(axis)
    return lax.ppermute(shard, axis, [(i, (i + by) % length) for i in range(length)])


def product(form, left, right):
    return jnp.einsum(form, left, right, precision=HIGH)


def select_send(sigma_local, row_blocks, slots):
    own_count = lax.axis_size("own")
    own_here = lax.axis_index("own")
    row_here = lax.axis_index("row")
    rows_here = sigma_local.shape[0] // B
    cols_here = sigma_local.shape[1] // B
    rowlist = row_blocks.reshape(own_count, slots, -1)
    group = own_here * cols_here // rows_here
    want_col = lax.dynamic_index_in_dim(rowlist, group, 2, keepdims=False)
    local_col = want_col - own_here * cols_here
    match = ((local_col >= 0) & (local_col < cols_here)).astype(jnp.int32)
    which = jnp.sum(match * jnp.arange(slots, dtype=jnp.int32)[None, :], axis=1)
    chosen = rowlist[jnp.arange(own_count, dtype=jnp.int32), which]
    chosen_row = (
        lax.dynamic_index_in_dim(chosen, row_here, 1, keepdims=False) - row_here * rows_here
    )
    chosen_col = jnp.clip(
        lax.dynamic_index_in_dim(chosen, group, 1, keepdims=False) - own_here * cols_here,
        0,
        cols_here - 1,
    )
    blocks4 = sigma_local.reshape(rows_here, B, cols_here, B)
    return blocks4[chosen_row, :, chosen_col, :]


def select_take(received, row_blocks, slots, cols_here):
    mine = lax.axis_index("own") * slots + jnp.arange(slots, dtype=jnp.int32)
    rowlist = row_blocks[mine]
    sender = rowlist // cols_here
    return received[sender]


def on_device(
    sigma_anc, row_blocks, panel1, diag_inv1, mask1, parent_block2, panel2, diag_inv2, mask2
):
    slots = panel1.shape[0]
    cols_here = sigma_anc.shape[1] // B
    keep_own2 = mask2.astype(jnp.float32)
    up_parent = product("kij,kjc->kic", parent_block2, diag_inv2)
    factor2_own = keep_own2[:, :, None] * product("kij,kjc->kic", panel2, diag_inv2)
    factor2_child = shifted(factor2_own, "own", -1)
    outgoing = select_send(sigma_anc, row_blocks, slots)
    received = lax.all_to_all(outgoing, "own", split_axis=0, concat_axis=0, tiled=True)
    blocks1 = select_take(received, row_blocks, slots, cols_here)
    keep1 = mask1.astype(jnp.float32)
    factor1 = keep1[:, :, None] * product("kij,kjc->kic", panel1, diag_inv1)
    factors1 = lax.all_gather(factor1, "row", axis=1, tiled=True).reshape(slots, -1, B, B)
    sel1_panel = -keep1[:, :, None] * product("kmij,kmjc->kic", blocks1, factors1)
    gram1 = product("kji,kjc->kic", diag_inv1, diag_inv1)
    sel1_diag = gram1 - lax.psum(product("kji,kjc->kic", factor1, sel1_panel), "row")
    factor2 = keep1[:, :, None] * factor2_child
    factors2 = lax.all_gather(factor2, "row", axis=1, tiled=True).reshape(slots, -1, B, B)
    anc2 = keep1[:, :, None] * product("kmij,kmjc->kic", blocks1, factors2)
    par_panel = shifted(sel1_panel, "own", 1)
    par_anc = shifted(anc2, "own", 1)
    par_diag = shifted(sel1_diag, "own", 1)
    sel2_panel = -keep_own2[:, :, None] * (product("kij,kjc->kic", par_panel, up_parent) + par_anc)
    cross = product("kji,kjc->kic", par_panel, factor2_own)
    back = product("kji,kjc->kic", factor2_own, sel2_panel)
    par_diag, cross, back = lax.optimization_barrier((par_diag, cross, back))
    cross, back = lax.psum((cross, back), "row")
    sel2_parent = -(product("kij,kjc->kic", par_diag, up_parent) + cross)
    gram2 = product("kji,kjc->kic", diag_inv2, diag_inv2)
    sel2_diag = gram2 - product("kji,kjc->kic", up_parent, sel2_parent) - back
    return (sel1_panel, sel1_diag, sel2_parent, sel2_panel, sel2_diag)


def solution(mesh):
    in_specs = (
        P("row", "own"),
        P(),
        P("own", "row", None),
        P("own", None, None),
        P("own", "row"),
        P("own", None, None),
        P("own", "row", None),
        P("own", None, None),
        P("own", "row"),
    )
    out_specs = (
        P("own", "row", None),
        P("own", None, None),
        P("own", None, None),
        P("own", "row", None),
        P("own", None, None),
    )
    return jax.shard_map(
        on_device, mesh=mesh, in_specs=in_specs, out_specs=out_specs, check_vma=False
    )
```

profile of v0, /device:TPU:2, one launch (start us, length us, event | category | flops | bytes accessed | tf_op | source)
XLA Modules:
  0.0 444.9 jit_solution(6164868798614665549)
XLA Ops:
  7.2 0.0 copy-start
  7.2 0.8 copy.67
  8.0 0.1 constant_dynamic-slice_fusion
  8.1 0.1 copy.90
  8.2 0.1 copy.69
  8.3 0.1 fusion.7
  8.5 0.7 gather_fusion
  9.1 5.9 %reshape.167 = f32[8,256,2,256]{3,2,1,0:T(2,128)} reshape(f32[2048,512]{1,0:T(8,128)} %param.9) | data formatting | bytes 8388608 | tf_op jit(solution)/shard_map/reshape | solution.py:40
  15.1 4.7 %copy.72 = f32[8,256,2,256]{3,1,2,0:T(8,128)} copy(f32[8,256,2,256]{3,2,1,0:T(2,128)} %reshape.167) | data formatting | bytes 8388608 | tf_op jit(solution)/shard_map/reshape | solution.py:40
  19.7 0.2 fusion.11
  19.9 6.5 %gather_fusion.1 = f32[32,256,256]{2,1,0:T(8,128)} fusion(f32[8,256,2,256]{3,1,2,0:T(8,128)} %copy.72, s32[32]{0:T(128)S(1)} %fusion.11), kind=kCustom, calls=%fused_computation.1 | custom fusion | bytes 16777472 | tf_op jit(solution)/shard_map/gather | solution.py:41
  26.5 11.8 %all-to-all-start = ((f32[32,256,256]{2,1,0:T(8,128)}), f32[32,256,256]{2,1,0:T(8,128)}, u32[]{:S(2)}, u32[]{:S(2)}) async-start(f32[32,256,256]{2,1,0:T(8,128)} %gather_fusion.1), calls=%async_computation | async-start | bytes 16777216 | tf_op jit(solution)/shard_map/all_to_all | solution.py:61
  38.3 0.0 all-gather.3.cloned.1.call-start
  38.4 1.5 convolution_multiply_fusion.1
  39.8 0.0 all-gather.3.cloned.1.call-update
  39.8 0.0 all-gather.5.cloned.1.call-start
  39.9 0.7 convolution_multiply_fusion
  40.6 2.8 collective-permute-start.2
  43.3 190.9 %collective-permute-done.2 = f32[2,256,256]{2,1,0:T(8,128)S(1)} collective-permute-done((f32[2,256,256]{2,1,0:T(8,128)S(1)}, f32[2,256,256]{2,1,0:T(8,128)S(1)}, u32[]{:S(2)}, u32[]{:S(2)}) %collective-permute-start.2) | collective-permute-done | bytes 524320 | tf_op jit(solution)/shard_map/ppermute | solution.py:12
  234.2 0.9 broadcast_multiply_fusion
  235.1 0.0 all-gather.5.cloned.1.call-update
  235.1 0.0 all-reduce.4.cloned.1.call-start
  235.2 0.6 gather_fusion.2
  235.8 0.1 reshape.158
  235.9 6.2 %gather_fusion.3 = f32[16,256,256]{2,1,0:T(8,128)} fusion(f32[32,256,256]{2,1,0:T(8,128)} %all-to-all-done, s32[1024]{0:T(1024)S(1)} %pad_clamp_fusion), kind=kCustom, calls=%fused_computation.3 | custom fusion | bytes 8388672 | tf_op jit(solution)/shard_map/gather | solution.py:48
  242.1 8.1 %fusion.3 = f32[2,256,256]{2,1,0:T(8,128)S(1)} fusion(f32[2,8,256,256]{3,2,1,0:T(8,128)} %bitcast.67, f32[2,8,256,256]{3,2,1,0:T(8,128)} %bitcast.69, f32[2]{0:T(128)S(1)} %fusion.16), kind=kOutput, calls=%fused_computation.14 | convolution fusion | flops 3221356544 | bytes 8912904 | tf_op jit(solution)/shard_map/kmij,kmjc->kic/dot_general | solution.py:16
  250.2 0.0 copy-start.3
  250.2 0.3 collective-permute-start.1
  250.5 1.9 fusion.18
  252.4 21.4 %all-gather.5.cloned.1.call-done = f32[2,2048,256]{2,1,0:T(8,128)} async-done(((f32[2,256,256]{2,1,0:T(8,128)}), f32[2,2048,256]{2,1,0:T(8,128)}) %all-gather.5.cloned.1.call-update) | async-done | bytes 4194320 | tf_op jit(solution)/shard_map/all_gather | solution.py:70
  273.8 8.2 %fusion.1 = f32[2,256,256]{2,1,0:T(8,128)} fusion(f32[2,8,256,256]{3,2,1,0:T(8,128)} %bitcast.68, f32[2,8,256,256]{3,2,1,0:T(8,128)} %bitcast.70, f32[2]{0:T(128)S(1)} %convert_bitcast_fusion.1), kind=kOutput, calls=%fused_computation.8 | convolution fusion | flops 3221356544 | bytes 8912904 | tf_op jit(solution)/shard_map/kmij,kmjc->kic/dot_general | solution.py:16
  282.0 1.5 collective-permute-start.3
  283.6 0.0 all-reduce.4.cloned.1.call-update
  283.6 0.0 all-reduce.6.cloned.1.call-start
  283.7 1.7 fusion.20
  285.4 63.5 %all-reduce.4.cloned.1.call-done = f32[2,256,256]{2,1,0:T(8,128)} async-done(((f32[2,256,256]{2,1,0:T(8,128)}), f32[2,256,256]{2,1,0:T(8,128)}) %all-reduce.4.cloned.1.call-update) | async-done | bytes 524304 | tf_op jit(solution)/shard_map/psum | solution.py:68
  348.9 2.9 convolution_subtract_fusion.1
  351.8 1.6 collective-permute-start
  353.3 1.7 fusion.2
  355.0 1.8 fusion.21
  356.9 1.8 fusion.19
  358.7 7.1 %collective-permute-done = f32[2,256,256]{2,1,0:T(8,128)} collective-permute-done((f32[2,256,256]{2,1,0:T(8,128)}, f32[2,256,256]{2,1,0:T(8,128)}, u32[]{:S(2)}, u32[]{:S(2)}) %collective-permute-start) | collective-permute-done | bytes 524320 | tf_op jit(solution)/shard_map/ppermute | solution.py:12
  365.8 0.0 all-reduce.6.cloned.1.call-update
  365.8 1.1 fusion.22
  366.9 67.6 %all-reduce.6.cloned.1.call-done = (f32[2,256,256]{2,1,0:T(8,128)}, f32[2,256,256]{2,1,0:T(8,128)}) async-done(((f32[2,256,256]{2,1,0:T(8,128)}, f32[2,256,256]{2,1,0:T(8,128)}), (f32[2,256,256]{2,1,0:T(8,128)}, f32[2,256,256]{2,1,0:T(8,128)})) %all-reduce.6.cloned.1.call-update) | async-done | bytes 1048592 | tf_op jit(solution)/shard_map/psum | solution.py:79
  434.5 1.9 fusion
  436.4 1.0 convolution_subtract_fusion
  437.5 0.9 sub.48
  (33 shorter events, 0.1 us)
Async XLA Ops:
  7.2 32.7 %copy-start = (f32[2,256,256]{2,1,0:T(8,128)S(1)}, f32[2,256,256]{2,1,0:T(8,128)}, u32[]{:S(2)}) copy-start(f32[2,256,256]{2,1,0:T(8,128)} %param.16) | copy-start | bytes 1572868
  26.4 11.9 %copy-start.9 = (s32[2,1]{0,1:T(1,128)S(1)}, s32[2,1]{0,1:T(1,128)}, u32[]{:S(2)}) copy-start(s32[2,1]{0,1:T(1,128)} %param.13) | copy-start | bytes 28
  26.4 11.9 %copy-start.2 = (f32[2,256,256]{2,1,0:T(8,128)S(1)}, f32[2,256,256]{2,1,0:T(8,128)}, u32[]{:S(2)}) copy-start(f32[2,256,256]{2,1,0:T(8,128)} %param.12) | copy-start | bytes 1572868
  26.4 11.9 %copy-start.7 = (f32[2,256,256]{2,1,0:T(8,128)S(1)}, f32[2,256,256]{2,1,0:T(8,128)}, u32[]{:S(2)}) copy-start(f32[2,256,256]{2,1,0:T(8,128)} %param.11) | copy-start | bytes 1572868
  26.4 13.5 %copy-start.10 = (s32[2,1]{0,1:T(1,128)S(1)}, s32[2,1]{0,1:T(1,128)}, u32[]{:S(2)}) copy-start(s32[2,1]{0,1:T(1,128)} %param.17) | copy-start | bytes 28
  26.4 13.5 %copy-start.8 = (f32[2,256,256]{2,1,0:T(8,128)S(1)}, f32[2,256,256]{2,1,0:T(8,128)}, u32[]{:S(2)}) copy-start(f32[2,256,256]{2,1,0:T(8,128)} %param.15) | copy-start | bytes 1572868
  26.5 209.4 %all-to-all-start = ((f32[32,256,256]{2,1,0:T(8,128)}), f32[32,256,256]{2,1,0:T(8,128)}, u32[]{:S(2)}, u32[]{:S(2)}) async-start(f32[32,256,256]{2,1,0:T(8,128)} %gather_fusion.1), calls=%async_computation | async-start | bytes 16777216 | tf_op jit(solution)/shard_map/all_to_all | solution.py:61
  38.3 203.8 %all-gather.3.cloned.1.call-start = ((), (), s32[]{:S(2)}) async-start(), calls=%async_computation.1 | async-start | bytes 4718592 | tf_op jit(solution)/shard_map/all_gather | solution.py:65
  39.8 234.0 %all-gather.5.cloned.1.call-start = ((), (), s32[]{:S(2)}) async-start(), calls=%async_computation.3 | async-start | bytes 4718592 | tf_op jit(solution)/shard_map/all_gather | solution.py:70
  40.6 193.6 %collective-permute-start.2 = (f32[2,256,256]{2,1,0:T(8,128)S(1)}, f32[2,256,256]{2,1,0:T(8,128)S(1)}, u32[]{:S(2)}, u32[]{:S(2)}) collective-permute-start(f32[2,256,256]{2,1,0:T(8,128)S(1)} %convolution_multiply_fusion), channel_id=1, source_target_pairs={{0,248},{8,0},{16,8},{24,16},{32,24},{40,32},{48,40},{56,48},{64,5... | collective-permute-start | bytes 1572872 | tf_op jit(solution)/shard_map/ppermute | solution.py:12
  235.1 113.7 %all-reduce.4.cloned.1.call-start = ((), (), s32[]{:S(2)}) async-start(), calls=%async_computation.2 | async-start | bytes 1048576 | tf_op jit(solution)/shard_map/psum | solution.py:68
  242.1 8.4 %copy-start.1 = (f32[2,256,256]{2,1,0:T(8,128)S(1)}, f32[2,256,256]{2,1,0:T(8,128)}, u32[]{:S(2)}) copy-start(f32[2,256,256]{2,1,0:T(8,128)} %convolution_multiply_fusion.1) | copy-start | bytes 1572868
  250.2 31.8 %copy-start.3 = (f32[2,256,256]{2,1,0:T(8,128)}, f32[2,256,256]{2,1,0:T(8,128)S(1)}, u32[]{:S(2)}) copy-start(f32[2,256,256]{2,1,0:T(8,128)S(1)} %fusion.3) | copy-start | bytes 1572868
  250.2 103.1 %collective-permute-start.1 = (f32[2,256,256]{2,1,0:T(8,128)S(1)}, f32[2,256,256]{2,1,0:T(8,128)S(1)}, u32[]{:S(2)}, u32[]{:S(2)}) collective-permute-start(f32[2,256,256]{2,1,0:T(8,128)S(1)} %fusion.3), channel_id=1, source_target_pairs={{0,8},{8,16},{16,24},{24,32},{32,40},{40,48},{48,56},{56,64},{64,7... | collective-permute-start | bytes 1572872 | tf_op jit(solution)/shard_map/ppermute | solution.py:12
  282.0 71.3 %collective-permute-start.3 = (f32[2,256,256]{2,1,0:T(8,128)}, f32[2,256,256]{2,1,0:T(8,128)}, u32[]{:S(2)}, u32[]{:S(2)}) collective-permute-start(f32[2,256,256]{2,1,0:T(8,128)} %fusion.1), channel_id=1, source_target_pairs={{0,8},{8,16},{16,24},{24,32},{32,40},{40,48},{48,56},{56,64},{64,7... | collective-permute-start | bytes 1572872 | tf_op jit(solution)/shard_map/ppermute | solution.py:12
  283.6 150.9 %all-reduce.6.cloned.1.call-start = ((), (), s32[]{:S(2)}) async-start(), calls=%async_computation.4 | async-start | bytes 2097152 | tf_op jit(solution)/shard_map/psum | solution.py:79
  351.8 14.1 %collective-permute-start = (f32[2,256,256]{2,1,0:T(8,128)}, f32[2,256,256]{2,1,0:T(8,128)}, u32[]{:S(2)}, u32[]{:S(2)}) collective-permute-start(f32[2,256,256]{2,1,0:T(8,128)} %convolution_subtract_fusion.1), channel_id=1, source_target_pairs={{0,8},{8,16},{16,24},{24,32},{32,40},{40,48},{48,56},{56,64},{64,7... | collective-permute-start | bytes 1572872 | tf_op jit(solution)/shard_map/ppermute | solution.py:12
  355.0 82.5 %copy-start.4 = (f32[2,256,256]{2,1,0:T(8,128)}, f32[2,256,256]{2,1,0:T(8,128)S(1)}, u32[]{:S(2)}) copy-start(f32[2,256,256]{2,1,0:T(8,128)S(1)} %fusion.2) | copy-start | bytes 1572868
  434.5 3.0 copy-start.6
  436.4 2.0 copy-start.5
Sparse Core Ops, SparseCore 0:
  41.5 35.7 all-gather.2
  235.3 38.5 all-gather.4
  283.7 65.0 all-reduce.3
  366.0 68.4 all-reduce.5
where the time goes:
time: 445 us
  waiting for transfers between devices  351 us (79%)
  matrix products  34.3 us (8%)
  local copies, waits for them, and re-layouts  25.7 us (6%)
  starting transfers between devices  18.1 us (4%)
  between operations  14 us (3%)
    ppermute x4, waiting for transfers between devices, shifted(): lax.ppermute(shard, axis, [(i, (i + by) % length) for i in range(length)])  198 us
    psum x1, waiting for transfers between devices, on_device(): cross, back = lax.psum((cross, back), 'row')  67.6 us
    psum x1, waiting for transfers between devices, on_device(): lax.psum(product('kji,kjc->kic', factor1, sel1_panel), 'row')  63.5 us
    dot_general x13, matrix products, product(): return jnp.einsum(form, left, right, precision=HIGH)  34.3 us
    all_gather x1, waiting for transfers between devices, on_device(): lax.all_gather(factor2, 'row', axis=1, tiled=True).reshape(slots, -1, B, B)  21.4 us
    all_to_all x1, starting transfers between devices, on_device(): lax.all_to_all(outgoing, 'own', split_axis=0, concat_axis=0, tiled=True)  11.8 us
    reshape x2, local copies, waits for them, and re-layouts, select_send(): blocks4 = sigma_local.reshape(rows_here, B, cols_here, B)  10.6 us
  transfers between devices with their start and end apart: 9, of which 5 were waited for; matrix products, arithmetic and copies ran while one was open for 9% of the time, Pallas kernels for 0%

commit v1 on v0

--- a/solution.py
+++ b/solution.py
@@ -67,7 +67,10 @@
     gram1 = product("kji,kjc->kic", diag_inv1, diag_inv1)
     sel1_diag = gram1 - lax.psum(product("kji,kjc->kic", factor1, sel1_panel), "row")
     factor2 = keep1[:, :, None] * factor2_child
-    factors2 = lax.all_gather(factor2, "row", axis=1, tiled=True).reshape(slots, -1, B, B)
+    divide_kinds = lambda w_in: jnp.concatenate(
+        lax.all_to_all(jnp.stack(lax.axis_size("row") * [w_in]), "row", 0, 0), axis=1
+    )
+    factors2 = divide_kinds(factor2).reshape(slots, -1, B, B)
     anc2 = keep1[:, :, None] * product("kmij,kmjc->kic", blocks1, factors2)
     par_panel = shifted(sel1_panel, "own", 1)
     par_anc = shifted(anc2, "own", 1)

time: 445 us -> 465 us (1.045)
  waiting for transfers between devices: 351 us -> 366 us
    all_to_all x0 -> x1, waiting for transfers between devices: none -> 32.5 us  [on_device(): lax.all_to_all(jnp.stack(lax.axis_size('row') * [w_in]), 'row', 0, 0)]
    all_gather x1 -> x0, waiting for transfers between devices: 21.4 us -> none  [on_device(): lax.all_gather(factor2, 'row', axis=1, tiled=True).reshape(slots, -1, B, B)]
where the time goes in v1:
time: 465 us; the launch traced here: 464 us
  waiting for transfers between devices  366 us (79%)
  matrix products  34.3 us (7%)
  local copies, waits for them, and re-layouts  28 us (6%)
  starting transfers between devices  21.1 us (5%)
  between operations  14 us (3%)
    ppermute x4, waiting for transfers between devices, shifted(): lax.ppermute(shard, axis, [(i, (i + by) % length) for i in range(length)])  198 us
    psum x1, waiting for transfers between devices, on_device(): cross, back = lax.psum((cross, back), 'row')  67.6 us
    psum x1, waiting for transfers between devices, on_device(): lax.psum(product('kji,kjc->kic', factor1, sel1_panel), 'row')  67.5 us
    dot_general x13, matrix products, product(): return jnp.einsum(form, left, right, precision=HIGH)  34.3 us
    all_to_all x1, waiting for transfers between devices, on_device(): lax.all_to_all(jnp.stack(lax.axis_size('row') * [w_in]), 'row', 0, 0)  32.5 us
    all_to_all x1, starting transfers between devices, on_device(): lax.all_to_all(outgoing, 'own', split_axis=0, concat_axis=0, tiled=True)  11.8 us
    reshape x2, local copies, waits for them, and re-layouts, select_send(): blocks4 = sigma_local.reshape(rows_here, B, cols_here, B)  10.5 us
  transfers between devices with their start and end apart: 9, of which 5 were waited for; matrix products, arithmetic and copies ran while one was open for 9% of the time, Pallas kernels for 0%

profile of v1, /device:TPU:2, one launch (start us, length us, event | category | flops | bytes accessed | tf_op | source)
XLA Modules:
  0.0 464.5 jit_solution(9643945245751888960)
XLA Ops:
  7.2 0.0 copy-start
  7.2 0.8 copy.83
  8.0 0.1 constant_dynamic-slice_fusion
  8.1 0.1 copy.107
  8.2 0.1 copy.85
  8.3 0.1 fusion.15
  8.5 0.7 gather_fusion
  9.1 5.9 %reshape.169 = f32[8,256,2,256]{3,2,1,0:T(2,128)} reshape(f32[2048,512]{1,0:T(8,128)} %param.9) | data formatting | bytes 8388608 | tf_op jit(solution)/shard_map/reshape | solution.py:40
  15.0 4.6 copy.88
  19.7 0.2 fusion.19
  19.9 6.5 %gather_fusion.1 = f32[32,256,256]{2,1,0:T(8,128)} fusion(f32[8,256,2,256]{3,1,2,0:T(8,128)} %copy.88, s32[32]{0:T(128)S(1)} %fusion.19), kind=kCustom, calls=%fused_computation.1 | custom fusion | bytes 16777472 | tf_op jit(solution)/shard_map/gather | solution.py:41
  26.4 11.8 %all-to-all-start = ((f32[32,256,256]{2,1,0:T(8,128)}), f32[32,256,256]{2,1,0:T(8,128)}, u32[]{:S(2)}, u32[]{:S(2)}) async-start(f32[32,256,256]{2,1,0:T(8,128)} %gather_fusion.1), calls=%async_computation | async-start | bytes 16777216 | tf_op jit(solution)/shard_map/all_to_all | solution.py:61
  38.2 0.0 all-gather.2.cloned.1.call-start
  38.3 1.5 convolution_multiply_fusion.1
  39.8 0.0 all-gather.2.cloned.1.call-update
  39.8 0.7 convolution_multiply_fusion
  40.5 2.7 collective-permute-start.2
  43.2 190.9 %collective-permute-done.2 = f32[2,256,256]{2,1,0:T(8,128)S(1)} collective-permute-done((f32[2,256,256]{2,1,0:T(8,128)S(1)}, f32[2,256,256]{2,1,0:T(8,128)S(1)}, u32[]{:S(2)}, u32[]{:S(2)}) %collective-permute-start.2) | collective-permute-done | bytes 524320 | tf_op jit(solution)/shard_map/ppermute | solution.py:12
  234.2 0.1 broadcast_multiply_fusion
  234.3 2.4 stack.2
  236.7 4.6 all-to-all-start.1
  241.3 0.0 all-reduce.4.cloned.1.call-start
  241.3 0.6 gather_fusion.2
  241.9 0.1 reshape.160
  242.0 6.1 %gather_fusion.3 = f32[16,256,256]{2,1,0:T(8,128)} fusion(f32[32,256,256]{2,1,0:T(8,128)} %all-to-all-done, s32[1024]{0:T(1024)S(1)} %pad_clamp_fusion), kind=kCustom, calls=%fused_computation.3 | custom fusion | bytes 8388672 | tf_op jit(solution)/shard_map/gather | solution.py:48
  248.1 8.1 %fusion.11 = f32[2,256,256]{2,1,0:T(8,128)S(1)} fusion(f32[2,8,256,256]{3,2,1,0:T(8,128)} %bitcast.72, f32[2,8,256,256]{3,2,1,0:T(8,128)} %bitcast.74, f32[2]{0:T(128)S(1)} %fusion.24), kind=kOutput, calls=%fused_computation.17 | convolution fusion | flops 3221356544 | bytes 8912904 | tf_op jit(solution)/shard_map/kmij,kmjc->kic/dot_general | solution.py:16
  256.3 0.0 copy-start.3
  256.3 0.3 collective-permute-start.1
  256.6 1.9 fusion.26
  258.4 32.5 %all-to-all-done.1 = f32[8,2,256,256]{3,2,1,0:T(8,128)} async-done(((f32[8,2,256,256]{3,2,1,0:T(8,128)}), f32[8,2,256,256]{3,2,1,0:T(8,128)}, u32[]{:S(2)}, u32[]{:S(2)}) %all-to-all-start.1) | async-done | bytes 4194336 | tf_op jit(solution)/shard_map/all_to_all | solution.py:71
  290.9 8.2 %fusion.6 = f32[2,256,256]{2,1,0:T(8,128)} fusion(f32[2,8,256,256]{3,2,1,0:T(8,128)} %bitcast.73, f32[8,2,256,256]{3,2,1,0:T(8,128)} %all-to-all-done.1, f32[2]{0:T(128)S(1)} %convert_bitcast_fusion.1), kind=kOutput, calls=%fused_computation.8 | convolution fusion | flops 3221356544 | bytes 8912904 | tf_op jit(solution)/shard_map/kmij,kmjc->kic/dot_general | solution.py:16
  299.2 0.0 all-reduce.4.cloned.1.call-update
  299.2 0.0 all-reduce.6.cloned.1.call-start
  299.2 1.7 fusion.28
  300.9 67.5 %all-reduce.4.cloned.1.call-done = f32[2,256,256]{2,1,0:T(8,128)} async-done(((f32[2,256,256]{2,1,0:T(8,128)}), f32[2,256,256]{2,1,0:T(8,128)}) %all-reduce.4.cloned.1.call-update) | async-done | bytes 524304 | tf_op jit(solution)/shard_map/psum | solution.py:68
  368.4 2.9 convolution_subtract_fusion.1
  371.3 1.6 collective-permute-start
  372.9 1.7 fusion.10
  374.6 1.8 fusion.29
  376.5 1.8 fusion.27
  378.3 7.1 %collective-permute-done = f32[2,256,256]{2,1,0:T(8,128)} collective-permute-done((f32[2,256,256]{2,1,0:T(8,128)}, f32[2,256,256]{2,1,0:T(8,128)}, u32[]{:S(2)}, u32[]{:S(2)}) %collective-permute-start) | collective-permute-done | bytes 524320 | tf_op jit(solution)/shard_map/ppermute | solution.py:12
  385.4 0.0 all-reduce.6.cloned.1.call-update
  385.4 1.1 fusion.30
  386.5 67.6 %all-reduce.6.cloned.1.call-done = (f32[2,256,256]{2,1,0:T(8,128)}, f32[2,256,256]{2,1,0:T(8,128)}) async-done(((f32[2,256,256]{2,1,0:T(8,128)}, f32[2,256,256]{2,1,0:T(8,128)}), (f32[2,256,256]{2,1,0:T(8,128)}, f32[2,256,256]{2,1,0:T(8,128)})) %all-reduce.6.cloned.1.call-update) | async-done | bytes 1048592 | tf_op jit(solution)/shard_map/psum | solution.py:82
  454.1 1.9 fusion.9
  456.0 0.0 copy-start.5
  456.0 1.0 convolution_subtract_fusion
  457.1 0.9 sub.48
  (33 shorter events, 0.1 us)
Async XLA Ops:
  7.2 32.7 %copy-start = (f32[2,256,256]{2,1,0:T(8,128)S(1)}, f32[2,256,256]{2,1,0:T(8,128)}, u32[]{:S(2)}) copy-start(f32[2,256,256]{2,1,0:T(8,128)} %param.16) | copy-start | bytes 1572868
  26.4 11.9 %copy-start.9 = (s32[2,1]{0,1:T(1,128)S(1)}, s32[2,1]{0,1:T(1,128)}, u32[]{:S(2)}) copy-start(s32[2,1]{0,1:T(1,128)} %param.13) | copy-start | bytes 28
  26.4 11.9 %copy-start.2 = (f32[2,256,256]{2,1,0:T(8,128)S(1)}, f32[2,256,256]{2,1,0:T(8,128)}, u32[]{:S(2)}) copy-start(f32[2,256,256]{2,1,0:T(8,128)} %param.12) | copy-start | bytes 1572868
  26.4 11.9 %copy-start.7 = (f32[2,256,256]{2,1,0:T(8,128)S(1)}, f32[2,256,256]{2,1,0:T(8,128)}, u32[]{:S(2)}) copy-start(f32[2,256,256]{2,1,0:T(8,128)} %param.11) | copy-start | bytes 1572868
  26.4 13.4 %copy-start.10 = (s32[2,1]{0,1:T(1,128)S(1)}, s32[2,1]{0,1:T(1,128)}, u32[]{:S(2)}) copy-start(s32[2,1]{0,1:T(1,128)} %param.17) | copy-start | bytes 28
  26.4 13.4 %copy-start.8 = (f32[2,256,256]{2,1,0:T(8,128)S(1)}, f32[2,256,256]{2,1,0:T(8,128)}, u32[]{:S(2)}) copy-start(f32[2,256,256]{2,1,0:T(8,128)} %param.15) | copy-start | bytes 1572868
  26.4 207.9 %all-to-all-start = ((f32[32,256,256]{2,1,0:T(8,128)}), f32[32,256,256]{2,1,0:T(8,128)}, u32[]{:S(2)}, u32[]{:S(2)}) async-start(f32[32,256,256]{2,1,0:T(8,128)} %gather_fusion.1), calls=%async_computation | async-start | bytes 16777216 | tf_op jit(solution)/shard_map/all_to_all | solution.py:61
  38.2 209.9 %all-gather.2.cloned.1.call-start = ((), (), s32[]{:S(2)}) async-start(), calls=%async_computation.2 | async-start | bytes 4718592 | tf_op jit(solution)/shard_map/all_gather | solution.py:65
  40.5 193.7 %collective-permute-start.2 = (f32[2,256,256]{2,1,0:T(8,128)S(1)}, f32[2,256,256]{2,1,0:T(8,128)S(1)}, u32[]{:S(2)}, u32[]{:S(2)}) collective-permute-start(f32[2,256,256]{2,1,0:T(8,128)S(1)} %convolution_multiply_fusion), channel_id=1, source_target_pairs={{0,248},{8,0},{16,8},{24,16},{32,24},{40,32},{48,40},{56,48},{64,5... | collective-permute-start | bytes 1572872 | tf_op jit(solution)/shard_map/ppermute | solution.py:12
  236.7 54.3 %all-to-all-start.1 = ((f32[8,2,256,256]{3,2,1,0:T(8,128)}), f32[8,2,256,256]{3,2,1,0:T(8,128)}, u32[]{:S(2)}, u32[]{:S(2)}) async-start(f32[8,2,256,256]{3,2,1,0:T(8,128)} %stack.2), calls=%async_computation.1 | async-start | bytes 8388608 | tf_op jit(solution)/shard_map/all_to_all | solution.py:71
  241.3 127.2 %all-reduce.4.cloned.1.call-start = ((), (), s32[]{:S(2)}) async-start(), calls=%async_computation.3 | async-start | bytes 1048576 | tf_op jit(solution)/shard_map/psum | solution.py:68
  248.1 8.4 %copy-start.1 = (f32[2,256,256]{2,1,0:T(8,128)S(1)}, f32[2,256,256]{2,1,0:T(8,128)}, u32[]{:S(2)}) copy-start(f32[2,256,256]{2,1,0:T(8,128)} %convolution_multiply_fusion.1) | copy-start | bytes 1572868
  256.3 42.9 %copy-start.3 = (f32[2,256,256]{2,1,0:T(8,128)}, f32[2,256,256]{2,1,0:T(8,128)S(1)}, u32[]{:S(2)}) copy-start(f32[2,256,256]{2,1,0:T(8,128)S(1)} %fusion.11) | copy-start | bytes 1572868
  256.3 116.6 %collective-permute-start.1 = (f32[2,256,256]{2,1,0:T(8,128)S(1)}, f32[2,256,256]{2,1,0:T(8,128)S(1)}, u32[]{:S(2)}, u32[]{:S(2)}) collective-permute-start(f32[2,256,256]{2,1,0:T(8,128)S(1)} %fusion.11), channel_id=1, source_target_pairs={{0,8},{8,16},{16,24},{24,32},{32,40},{40,48},{48,56},{56,64},{64,7... | collective-permute-start | bytes 1572872 | tf_op jit(solution)/shard_map/ppermute | solution.py:12
  299.2 73.7 %collective-permute-start.3 = (f32[2,256,256]{2,1,0:T(8,128)}, f32[2,256,256]{2,1,0:T(8,128)}, u32[]{:S(2)}, u32[]{:S(2)}) collective-permute-start(f32[2,256,256]{2,1,0:T(8,128)} %fusion.6), channel_id=1, source_target_pairs={{0,8},{8,16},{16,24},{24,32},{32,40},{40,48},{48,56},{56,64},{64,7... | collective-permute-start | bytes 1572872 | tf_op jit(solution)/shard_map/ppermute | solution.py:12
  299.2 154.9 %all-reduce.6.cloned.1.call-start = ((), (), s32[]{:S(2)}) async-start(), calls=%async_computation.4 | async-start | bytes 2097152 | tf_op jit(solution)/shard_map/psum | solution.py:82
  371.3 14.1 %collective-permute-start = (f32[2,256,256]{2,1,0:T(8,128)}, f32[2,256,256]{2,1,0:T(8,128)}, u32[]{:S(2)}, u32[]{:S(2)}) collective-permute-start(f32[2,256,256]{2,1,0:T(8,128)} %convolution_subtract_fusion.1), channel_id=1, source_target_pairs={{0,8},{8,16},{16,24},{24,32},{32,40},{40,48},{48,56},{56,64},{64,7... | collective-permute-start | bytes 1572872 | tf_op jit(solution)/shard_map/ppermute | solution.py:12
  374.6 82.5 %copy-start.4 = (f32[2,256,256]{2,1,0:T(8,128)}, f32[2,256,256]{2,1,0:T(8,128)S(1)}, u32[]{:S(2)}) copy-start(f32[2,256,256]{2,1,0:T(8,128)S(1)} %fusion.10) | copy-start | bytes 1572868
  454.1 3.0 copy-start.6
  456.0 2.0 copy-start.5
Sparse Core Ops, SparseCore 0:
  41.5 35.7 all-gather.1
  299.3 69.0 all-reduce.3
  385.5 68.4 all-reduce.5
